TPU v7x, 32 devices: a whole 2x2x4 slice. The times are simulated.
32 devices in a mesh: slab: 8 (over y, x, core), pencil: 4 (over z).
Axes of the slice: x: 2, y: 2, z: 4, core: 2. Of those that a mesh axis runs over, the one named last changes fastest.
Arguments:
- descriptors: bfloat16 [49152, 1600], P(('slab', 'pencil')), may hold values from -6 to 6
- species: int32 [49152], P(('slab', 'pencil')), may hold values from 0 to 3
- bucket_count: int32 [128], P(('slab', 'pencil')), may hold values from 288 to 384, as said below
- base_index: int32 [3, 49152], P(None, ('slab', 'pencil')), may hold values from 0 to 383, as said below
- fraction: float32 [3, 49152], P(None, ('slab', 'pencil')), may hold values from 0 to 0.999
- weight_in: bfloat16 [1600, 256], replicated, may hold values from -0.15625 to 0.15625
- bias_in: float32 [256], replicated, may hold values from -4 to 4
- weight_mid: bfloat16 [2, 256, 256], replicated, may hold values from -0.375 to 0.375
- bias_mid: float32 [2, 256], replicated, may hold values from -4 to 4
- weight_out: bfloat16 [3, 256], replicated, may hold values from -0.0390625 to 0.0390625
- bias_out: float32 [3], replicated, may hold values from -0.2 to 0.2
Outputs:
- energy: float32 [], replicated
- site_forces: float32 [2, 3, 49152], P(None, None, ('slab', 'pencil'))
- descriptor_grad: bfloat16 [49152, 1600], P(('slab', 'pencil'))
Inputs may be any that keep to these rules, and one draw needn't show every extreme that they name: Slot i is in use when i % 384 < bucket_count[i // 384]. Among the buckets of every device at least one is full. Slots come in blocks of 1536; block d belongs to slab index d // 4 and pencil index d % 4. base_index[0, i] lies in that slab's planes, within the 4 planes of the slot's bucket (bucket b covers that slab's planes (b % 4) * 4 onwards); base_index[1, i] lies in that pencil's 48 rows; base_index[2, i] is any column.
All inputs are finite; a program needn't handle non-finite values.
Results may differ from a plain program's by a relative error of at most 0.018.
Values sent between devices are 32-bit elements; how exact they have to be, the bound alone decides.
No kernel may reach another device: no remote copies, remote signals or barrier semaphores. Data moves between devices by JAX's collectives and lax.ppermute only.
A program may use at most 192 MiB of HBM per device.

v0:
```python
import math
import jax
import jax.numpy as jnp
from jax import lax
from jax.sharding import PartitionSpec as P

NX = 384
CZ = 16
CY = 48
BZ = 4
ion_table = (6.0, 1.0, 9.0, 7.0)
wannier_table = (-8.0, 0.0, -8.0, -8.0)
spline_coeffs = (1.0 / 120.0, 26.0 / 120.0, 66.0 / 120.0, 26.0 / 120.0, 1.0 / 120.0)
ewald_beta = 1.4
shift_scale = 0.9
highest = lax.Precision.HIGHEST


def extended(cells, sides, width):
    for axis, dim in sides:
        count = lax.axis_size(axis)
        head = lax.slice_in_dim(cells, 0, width, axis=dim)
        tail = lax.slice_in_dim(cells, cells.shape[dim] - width, cells.shape[dim], axis=dim)
        cells = jnp.concatenate(
            [
                lax.ppermute(tail, axis, [(i, (i + 1) % count) for i in range(count)]),
                cells,
                lax.ppermute(head, axis, [((i + 1) % count, i) for i in range(count)]),
            ],
            axis=dim,
        )
    return cells


def bspline(offset):
    folded = jnp.minimum(offset, 6.0 - offset)
    part_one = jnp.maximum(folded, 0.0)
    part_two = jnp.maximum(folded - 1.0, 0.0)
    part_three = jnp.maximum(folded - 2.0, 0.0)
    spline_val = (part_one**5 - 6.0 * part_two**5 + 15.0 * part_three**5) / 120.0
    spline_slope = (part_one**4 - 6.0 * part_two**4 + 15.0 * part_three**4) / 24.0
    return (spline_val, jnp.where(offset <= 3.0, spline_slope, -spline_slope))


def species_charge(species, charge_list):
    kind_ids = jnp.arange(len(charge_list), dtype=jnp.int32)
    levels = jnp.asarray(charge_list, jnp.float32)
    picked = jnp.where(species[None, :] == kind_ids[:, None], levels[:, None], 0.0)
    return jnp.sum(picked, axis=0)


def fitting(descriptors, weight_in, bias_in, weight_mid, bias_mid, weight_out, bias_out):
    hidden = jnp.tanh(
        jnp.dot(descriptors, weight_in, preferred_element_type=jnp.float32) + bias_in
    ).astype(jnp.bfloat16)
    for layer_idx in range(weight_mid.shape[0]):
        pre_act = (
            jnp.dot(hidden, weight_mid[layer_idx], preferred_element_type=jnp.float32)
            + bias_mid[layer_idx]
        )
        hidden = (hidden.astype(jnp.float32) + jnp.tanh(pre_act)).astype(jnp.bfloat16)
    output_raw = lax.dot_general(
        weight_out, hidden, (((1,), (1,)), ((), ())), preferred_element_type=jnp.float32
    )
    return shift_scale * jnp.tanh(output_raw + bias_out[:, None])


def axis_terms(index, length):
    signed = jnp.where(2 * index >= length, index - length, index).astype(jnp.float32) / length
    orders = jnp.arange(1, 6, dtype=jnp.int32)
    phases = (index[:, None] * orders[None, :] % length).astype(jnp.float32) * (
        2.0 * math.pi / length
    )
    coeffs = jnp.asarray(spline_coeffs, jnp.float32)
    real_sum = jnp.sum(coeffs[None, :] * jnp.cos(phases), axis=1)
    imag_sum = jnp.sum(coeffs[None, :] * jnp.sin(phases), axis=1)
    modulus = 1.0 / (real_sum * real_sum + imag_sum * imag_sum)
    damping = jnp.exp(-((math.pi / ewald_beta) ** 2) * signed * signed)
    return (signed * signed, damping * modulus)


def influence(z_index, z_len, y_index, y_len, x_index, x_len):
    z_sq, z_fac = axis_terms(z_index, z_len)
    y_sq, y_fac = axis_terms(y_index, y_len)
    x_sq, x_fac = axis_terms(x_index, x_len)
    squared = z_sq[:, None, None] + y_sq[None, :, None] + x_sq[None, None, :]
    safe_sq = jnp.where(squared > 0.0, squared, 1.0)
    volume = float(z_len * y_len * x_len)
    scaled = (
        z_fac[:, None, None]
        * y_fac[None, :, None]
        * x_fac[None, None, :]
        / (math.pi * volume * safe_sq)
    )
    return jnp.where(squared > 0.0, scaled, 0.0)


def dft_table(length):
    index = jnp.arange(length, dtype=jnp.int32)
    angles = (index[:, None] * index[None, :] % length).astype(jnp.float32) * (
        2.0 * math.pi / length
    )
    return (jnp.cos(angles), jnp.sin(angles))


def half_table(length, width):
    positions = jnp.arange(length, dtype=jnp.int32)
    wave_ids = jnp.arange(width, dtype=jnp.int32)
    angles = (positions[:, None] * wave_ids[None, :] % length).astype(jnp.float32) * (
        2.0 * math.pi / length
    )
    kept_mask = (2 * wave_ids <= length).astype(jnp.float32)
    doubled = (
        jnp.where((wave_ids == 0) | (2 * wave_ids == length), 1.0, 2.0).astype(jnp.float32)
        * kept_mask
    )
    return (jnp.cos(angles) * kept_mask[None, :], jnp.sin(angles) * kept_mask[None, :], doubled)


def dense_window(relative, start, length):
    steps_idx = jnp.arange(8, dtype=jnp.int32)
    spline_val, spline_slope = bspline(
        relative[:, None] - steps_idx.astype(jnp.float32)[None, :] + 6.0
    )
    cell_ids = jnp.arange(length, dtype=jnp.int32)
    target = (start[:, None] + steps_idx[None, :]) % length
    matches = target[:, :, None] == cell_ids[None, None, :]
    dense_val = jnp.sum(jnp.where(matches, spline_val[:, :, None], 0.0), axis=1)
    dense_slope = jnp.sum(jnp.where(matches, spline_slope[:, :, None], 0.0), axis=1)
    return (dense_val, dense_slope)


def lead_product(table, data, dim):
    return lax.dot_general(table, data, (((1,), (dim,)), ((), ())), precision=highest)


def forward_pair(cosine, sine, real_part, imag_part, dim):
    real_cos = lead_product(cosine, real_part, dim)
    imag_sin = lead_product(sine, imag_part, dim)
    imag_cos = lead_product(cosine, imag_part, dim)
    real_sin = lead_product(sine, real_part, dim)
    return (real_cos + imag_sin, imag_cos - real_sin)


def inverse_pair(cosine, sine, real_part, imag_part, dim):
    real_cos = lead_product(cosine, real_part, dim)
    imag_sin = lead_product(sine, imag_part, dim)
    imag_cos = lead_product(cosine, imag_part, dim)
    real_sin = lead_product(sine, real_part, dim)
    return (real_cos - imag_sin, real_sin + imag_cos)


def body(
    descriptors,
    species,
    bucket_count,
    base_index,
    fraction,
    weight_in,
    bias_in,
    weight_mid,
    bias_mid,
    weight_out,
    bias_out,
):
    n_slab = lax.axis_size("slab")
    n_pencil = lax.axis_size("pencil")
    slab_idx = lax.axis_index("slab")
    pencil_idx = lax.axis_index("pencil")
    rows_all = CY * n_pencil
    planes_all = CZ * n_slab
    row_part = rows_all // n_slab
    half_cols = NX // 2 + 1
    wave_cols = -(-half_cols // n_pencil) * n_pencil
    column_part = wave_cols // n_pencil
    n_buckets = bucket_count.shape[0]
    capacity = species.shape[0] // n_buckets
    site_count = 2 * capacity
    slot_ids = jnp.arange(capacity, dtype=jnp.int32)
    in_use = (slot_ids[None, :] < bucket_count[:, None]).reshape(-1).astype(jnp.float32)
    charges = (
        jnp.stack([species_charge(species, ion_table), species_charge(species, wannier_table)])
        * in_use[None, :]
    )

    def network(features):
        return fitting(features, weight_in, bias_in, weight_mid, bias_mid, weight_out, bias_out)

    centroid_shift, pullback = jax.vjp(network, descriptors)
    relative = jnp.stack([fraction, fraction + centroid_shift])
    anchor = jnp.stack([slab_idx * CZ, pencil_idx * CY, jnp.zeros((), jnp.int32)])
    local_base = base_index - anchor[:, None]
    site_charge = (
        charges.reshape(2, n_buckets, capacity).transpose(1, 0, 2).reshape(n_buckets, site_count)
    )
    site_rel = (
        relative.reshape(2, 3, n_buckets, capacity)
        .transpose(2, 1, 0, 3)
        .reshape(n_buckets, 3, site_count)
    )
    site_base = jnp.broadcast_to(
        local_base.reshape(3, n_buckets, 1, capacity), (3, n_buckets, 2, capacity)
    )
    site_base = site_base.transpose(1, 0, 2, 3).reshape(n_buckets, 3, site_count)
    bucket_ids = jnp.arange(n_buckets, dtype=jnp.int32)
    window_shape = (BZ + 8, CY + 8, NX)
    zero_index = jnp.zeros((), jnp.int32)

    def spread_step(grid_now, inputs):
        bucket, charge, rel_pos, base_pos = inputs
        plane_val, plane_slope = dense_window(rel_pos[0], base_pos[0] - bucket * BZ + 1, BZ + 8)
        row_val, row_slope = dense_window(rel_pos[1], base_pos[1] + 1, CY + 8)
        col_val, col_slope = dense_window(rel_pos[2], base_pos[2] - 3, NX)
        outer_prod = ((charge[:, None] * plane_val)[:, :, None] * row_val[:, None, :]).reshape(
            site_count, -1
        )
        block_sum = lax.dot_general(
            outer_prod, col_val, (((0,), (0,)), ((), ())), precision=highest
        )
        corner = (bucket * BZ, zero_index, zero_index)
        current = lax.dynamic_slice(grid_now, corner, window_shape)
        grid_now = lax.dynamic_update_slice(
            grid_now, current + block_sum.reshape(window_shape), corner
        )
        return (grid_now, (plane_val, plane_slope, row_val, row_slope, col_val, col_slope))

    charge_grid, windows = lax.scan(
        spread_step,
        jnp.zeros((CZ + 8, CY + 8, NX), jnp.float32),
        (bucket_ids, site_charge, site_rel, site_base),
    )
    half_cos, half_sin, doubled = half_table(NX, wave_cols)
    forward_rows = jnp.stack([half_cos.T, -half_sin.T], axis=1).reshape(2 * wave_cols, NX)
    inverse_rows = jnp.stack(
        [(half_cos * doubled[None, :]).T, (-half_sin * doubled[None, :]).T], axis=0
    )
    row_cos, row_sin = dft_table(rows_all)
    plane_cos, plane_sin = dft_table(planes_all)
    rim_planes = jnp.concatenate([charge_grid[:4], charge_grid[CZ + 4 :]], axis=0)
    arrived = extended(rim_planes, (("slab", 0),), 4)
    inner_grid = charge_grid[4 : CZ + 4].at[:4].add(arrived[:4]).at[CZ - 4 :].add(arrived[12:])
    rim_rows = jnp.concatenate([inner_grid[:, :4], inner_grid[:, CY + 4 :]], axis=1)
    arrived = extended(rim_rows, (("pencil", 1),), 4)
    source_grid = (
        inner_grid[:, 4 : CY + 4].at[:, :4].add(arrived[:, :4]).at[:, CY - 4 :].add(arrived[:, 12:])
    )
    plane_here = source_grid.shape[0]
    row_here = source_grid.shape[1]
    spectrum = lead_product(forward_rows, source_grid, 2).reshape(
        wave_cols, 2, plane_here, row_here
    )
    spectrum = lax.all_to_all(spectrum, "pencil", split_axis=0, concat_axis=3, tiled=True)
    real_y, imag_y = forward_pair(row_cos, row_sin, spectrum[:, 0], spectrum[:, 1], 2)
    spectrum = jnp.stack([real_y, imag_y], axis=1)
    spectrum = lax.all_to_all(spectrum, "slab", split_axis=0, concat_axis=3, tiled=True)
    real_z, imag_z = forward_pair(plane_cos, plane_sin, spectrum[:, 0], spectrum[:, 1], 2)
    x_ids = pencil_idx * column_part + jnp.arange(column_part, dtype=jnp.int32)
    factor = influence(
        jnp.arange(planes_all, dtype=jnp.int32),
        planes_all,
        slab_idx * row_part + jnp.arange(row_part, dtype=jnp.int32),
        rows_all,
        x_ids,
        NX,
    )
    weighted_real = real_z * factor
    weighted_imag = imag_z * factor
    power = weighted_real * real_z + weighted_imag * imag_z
    x_weight = jnp.where((x_ids == 0) | (2 * x_ids == NX), 1.0, 2.0).astype(jnp.float32)
    x_weight = x_weight * (2 * x_ids <= NX).astype(jnp.float32)
    energy_terms = 0.5 * jnp.sum(power * x_weight)
    energy_sum = lax.psum(energy_terms, ("slab", "pencil"))
    back_real, back_imag = inverse_pair(plane_cos, plane_sin, weighted_real, weighted_imag, 0)
    returned = jnp.stack([back_real, back_imag], axis=1)
    returned = lax.all_to_all(returned, "slab", split_axis=0, concat_axis=2, tiled=True)
    back_real, back_imag = inverse_pair(row_cos, row_sin, returned[:, 0], returned[:, 1], 1)
    returned = jnp.stack([back_real, back_imag], axis=1)
    returned = lax.all_to_all(returned, "pencil", split_axis=0, concat_axis=3, tiled=True)
    potential = lax.dot_general(
        returned, inverse_rows, (((1, 3), (0, 1)), ((), ())), precision=highest
    )
    potential = extended(potential, (("slab", 1), ("pencil", 0)), 4)

    def sample_step(inputs):
        bucket, plane_val, plane_slope, row_val, row_slope, col_val, col_slope = inputs
        corner = (zero_index, bucket * BZ, zero_index)
        patch = lax.dynamic_slice(potential, corner, (CY + 8, BZ + 8, NX)).reshape(-1, NX)
        stacked = jnp.concatenate([col_val, col_slope], axis=0)
        both = lax.dot_general(stacked, patch, (((1,), (1,)), ((), ())), precision=highest)
        along = both[:site_count].reshape(site_count, CY + 8, BZ + 8)
        across = both[site_count:].reshape(site_count, CY + 8, BZ + 8)
        site_level = jnp.einsum("sz,sy,syz->s", plane_val, row_val, along, precision=highest)
        grad_z = jnp.einsum("sz,sy,syz->s", plane_slope, row_val, along, precision=highest)
        grad_y = jnp.einsum("sz,sy,syz->s", plane_val, row_slope, along, precision=highest)
        grad_x = jnp.einsum("sz,sy,syz->s", plane_val, row_val, across, precision=highest)
        return (site_level, jnp.stack([grad_z, grad_y, grad_x]))

    levels, slopes = lax.map(sample_step, (bucket_ids,) + tuple(windows))
    forces = -site_charge[:, None, :] * slopes
    site_forces = forces.reshape(n_buckets, 3, 2, capacity).transpose(2, 1, 0, 3).reshape(2, 3, -1)
    (descriptor_grad,) = pullback(-site_forces[1])
    total_slots = species.shape[0] * n_slab * n_pencil
    energy = energy_sum / float(total_slots)
    return (energy, site_forces, descriptor_grad)


def solution(mesh):
    in_specs = (
        P(("slab", "pencil"), None),
        P(("slab", "pencil")),
        P(("slab", "pencil")),
        P(None, ("slab", "pencil")),
        P(None, ("slab", "pencil")),
        P(),
        P(),
        P(),
        P(),
        P(),
        P(),
    )
    out_specs = (P(), P(None, None, ("slab", "pencil")), P(("slab", "pencil"), None))
    return jax.shard_map(body, mesh=mesh, in_specs=in_specs, out_specs=out_specs, check_vma=False)
```

profile of v0, /device:TPU:12, one launch (start us, length us, event | category | flops | bytes accessed | tf_op | source)
XLA Modules:
  0.0 749.2 jit_solution(451744507878971859)
XLA Ops:
  13.4 99.9 %while.39 = (s32[]{:T(128)}, f32[24,56,384]{2,1,0:T(8,128)}, f32[4,768,12]{1,2,0:T(8,128)S(1)}, f32[4,768,12]{1,2,0:T(8,128)}, f32[4,768,56]{1,2,0:T(8,128)}, /*...) while((s32[]{:T(128)}, f32[24,56,384]{2,1,0:T(8,128)}, ...), condition=%wide.region_9.10_spmd, body=%wide.region_2.9_spmd.sunk | while | flops 2392848384 | bytes 12563475 | solution.py:227
  15.5 13.0 %select_reduce_fusion.11 = (f32[768,384]{1,0:T(8,128)S(1)}, f32[768,384]{1,0:T(8,128)S(1)}) fusion(f32[768,8]{1,0:T(8,128)S(1)} %copy.162, s32[768,8]{1,0:T(8,128)S(1)} %copy.163, f32[768,8]{1,0:T(8,128)S(1)} %copy.164), kind=kLoop, calls=%fused_computation.17.clone.1 | loop fusion | flops 11206656 | bytes 2433024 | tf_op jit(solution)/shard_map/while/body/eval_jaxpr/reduce_sum | solution.py:129
  40.4 13.0 %select_reduce_fusion.11 = (f32[768,384]{1,0:T(8,128)S(1)}, f32[768,384]{1,0:T(8,128)S(1)}) fusion(f32[768,8]{1,0:T(8,128)S(1)} %copy.162, s32[768,8]{1,0:T(8,128)S(1)} %copy.163, f32[768,8]{1,0:T(8,128)S(1)} %copy.164), kind=kLoop, calls=%fused_computation.17.clone.1 | loop fusion | flops 11206656 | bytes 2433024 | tf_op jit(solution)/shard_map/while/body/eval_jaxpr/reduce_sum | solution.py:129
  65.4 13.0 %select_reduce_fusion.11 = (f32[768,384]{1,0:T(8,128)S(1)}, f32[768,384]{1,0:T(8,128)S(1)}) fusion(f32[768,8]{1,0:T(8,128)S(1)} %copy.162, s32[768,8]{1,0:T(8,128)S(1)} %copy.163, f32[768,8]{1,0:T(8,128)S(1)} %copy.164), kind=kLoop, calls=%fused_computation.17.clone.1 | loop fusion | flops 11206656 | bytes 2433024 | tf_op jit(solution)/shard_map/while/body/eval_jaxpr/reduce_sum | solution.py:129
  90.4 13.0 %select_reduce_fusion.11 = (f32[768,384]{1,0:T(8,128)S(1)}, f32[768,384]{1,0:T(8,128)S(1)}) fusion(f32[768,8]{1,0:T(8,128)S(1)} %copy.162, s32[768,8]{1,0:T(8,128)S(1)} %copy.163, f32[768,8]{1,0:T(8,128)S(1)} %copy.164), kind=kLoop, calls=%fused_computation.17.clone.1 | loop fusion | flops 11206656 | bytes 2433024 | tf_op jit(solution)/shard_map/while/body/eval_jaxpr/reduce_sum | solution.py:129
  151.8 23.2 %all-to-all-done = f32[4,1,75264]{2,1,0:T(1,128)S(1)} async-done(((f32[4,1,75264]{2,1,0:T(1,128)}), f32[4,1,75264]{2,1,0:T(1,128)S(1)}, u32[]{:S(2)}, u32[]{:S(2)}) %all-to-all-start) | async-done | bytes 1204256 | tf_op jit(solution)/shard_map/all_to_all | solution.py:252
  189.4 11.7 %all_to_all.55 = f32[49,2,16,192]{3,2,1,0:T(8,128)S(1)} reshape(f32[49,2,16,4,48]{4,3,2,1,0:T(4,128)} %bitcast.337) | data formatting | bytes 2408448 | tf_op jit(solution)/shard_map/all_to_all | solution.py:252
  224.2 15.1 %all-to-all-done.1 = f32[8,1,37632]{2,1,0:T(1,128)S(1)} async-done(((f32[8,1,37632]{2,1,0:T(1,128)}), f32[8,1,37632]{2,1,0:T(1,128)S(1)}, u32[]{:S(2)}, u32[]{:S(2)}) %all-to-all-start.1) | async-done | bytes 1204256 | tf_op jit(solution)/shard_map/all_to_all | solution.py:255
  274.5 19.4 %all_to_all.72 = f32[8,1,37632]{2,1,0:T(1,128)S(1)} all-to-all(f32[8,1,37632]{2,1,0:T(1,128)S(1)} %reshape.1135), channel_id=1, replica_groups=mesh['slab'=8,'pencil'=4] {'slab'}, dimensions={0} | all-to-all | bytes 2408448 | tf_op jit(solution)/shard_map/all_to_all | solution.py:275
  336.6 23.8 %all-to-all-done.3 = f32[4,1,75264]{2,1,0:T(1,128)S(1)} async-done(((f32[4,1,75264]{2,1,0:T(1,128)}), f32[4,1,75264]{2,1,0:T(1,128)S(1)}, u32[]{:S(2)}, u32[]{:S(2)}) %all-to-all-start.3) | async-done | bytes 1204256 | tf_op jit(solution)/shard_map/all_to_all | solution.py:278
  399.1 44.4 %psum.7 = f32[]{:T(128)} all-reduce(f32[]{:T(128)S(6)} %mul_shard_map.3), channel_id=1, replica_groups=mesh['slab'=8,'pencil'=4] {'slab','pencil'}, use_global_device_ids=true, to_apply=%region_17.18 | all-reduce | flops 1 | bytes 8 | tf_op jit(solution)/shard_map/psum | solution.py:272
  445.8 293.6 %while.40 = (s32[]{:T(128)}, f32[4,3,768]{2,1,0:T(4,128)S(1)}, f32[4,768,12]{1,2,0:T(8,128)}, f32[4,768,56]{1,2,0:T(8,128)}, f32[4,768,384]{2,1,0:T(8,128)}, /*i...) while((s32[]{:T(128)}, f32[4,3,768]{2,1,0:T(4,128)S(1)}, ...), condition=%wide.region_19.20_spmd, body=%wide.region_18.19_spmd.sunk | while | flops 4775567872 | bytes 50012400 | solution.py:298
  472.0 12.6 %fusion.369 = f32[768,1,12]{2,1,0:T(1,128)} fusion(f32[768,56,1]{1,2,0:T(1,128)S(1)} %bitcast.322, f32[768,56,12]{1,2,0:T(8,128)} %copy.169), kind=kOutput, calls=%fused_computation.446.clone.1 | convolution fusion | flops 6193152 | bytes 2273280 | tf_op jit(solution)/shard_map/while/body/eval_jaxpr/sz,sy,syz->s/dot_general | solution.py:295
  493.6 12.0 %fusion.368 = f32[768,1,12]{2,1,0:T(1,128)S(1)} fusion(f32[768,56,1]{1,2,0:T(1,128)S(1)} %bitcast.325, f32[768,56,12]{1,2,0:T(8,128)} %copy.167), kind=kOutput, calls=%fused_computation.445.clone.1 | convolution fusion | flops 6193152 | bytes 2273280 | tf_op jit(solution)/shard_map/while/body/eval_jaxpr/sz,sy,syz->s/dot_general | solution.py:294
  507.0 12.0 %fusion.370 = f32[768,1,12]{2,1,0:T(1,128)S(1)} fusion(f32[768,56,1]{1,2,0:T(1,128)S(1)} %bitcast.323, f32[768,56,12]{1,2,0:T(8,128)} %copy.167), kind=kOutput, calls=%fused_computation.444.clone.1 | convolution fusion | flops 6193152 | bytes 2273280 | tf_op jit(solution)/shard_map/while/body/eval_jaxpr/sz,sy,syz->s/dot_general | solution.py:293
  545.4 12.6 %fusion.369 = f32[768,1,12]{2,1,0:T(1,128)} fusion(f32[768,56,1]{1,2,0:T(1,128)S(1)} %bitcast.322, f32[768,56,12]{1,2,0:T(8,128)} %copy.169), kind=kOutput, calls=%fused_computation.446.clone.1 | convolution fusion | flops 6193152 | bytes 2273280 | tf_op jit(solution)/shard_map/while/body/eval_jaxpr/sz,sy,syz->s/dot_general | solution.py:295
  567.0 12.0 %fusion.368 = f32[768,1,12]{2,1,0:T(1,128)S(1)} fusion(f32[768,56,1]{1,2,0:T(1,128)S(1)} %bitcast.325, f32[768,56,12]{1,2,0:T(8,128)} %copy.167), kind=kOutput, calls=%fused_computation.445.clone.1 | convolution fusion | flops 6193152 | bytes 2273280 | tf_op jit(solution)/shard_map/while/body/eval_jaxpr/sz,sy,syz->s/dot_general | solution.py:294
  580.4 12.0 %fusion.370 = f32[768,1,12]{2,1,0:T(1,128)S(1)} fusion(f32[768,56,1]{1,2,0:T(1,128)S(1)} %bitcast.323, f32[768,56,12]{1,2,0:T(8,128)} %copy.167), kind=kOutput, calls=%fused_computation.444.clone.1 | convolution fusion | flops 6193152 | bytes 2273280 | tf_op jit(solution)/shard_map/while/body/eval_jaxpr/sz,sy,syz->s/dot_general | solution.py:293
  618.6 12.6 %fusion.369 = f32[768,1,12]{2,1,0:T(1,128)} fusion(f32[768,56,1]{1,2,0:T(1,128)S(1)} %bitcast.322, f32[768,56,12]{1,2,0:T(8,128)} %copy.169), kind=kOutput, calls=%fused_computation.446.clone.1 | convolution fusion | flops 6193152 | bytes 2273280 | tf_op jit(solution)/shard_map/while/body/eval_jaxpr/sz,sy,syz->s/dot_general | solution.py:295
  640.2 12.0 %fusion.368 = f32[768,1,12]{2,1,0:T(1,128)S(1)} fusion(f32[768,56,1]{1,2,0:T(1,128)S(1)} %bitcast.325, f32[768,56,12]{1,2,0:T(8,128)} %copy.167), kind=kOutput, calls=%fused_computation.445.clone.1 | convolution fusion | flops 6193152 | bytes 2273280 | tf_op jit(solution)/shard_map/while/body/eval_jaxpr/sz,sy,syz->s/dot_general | solution.py:294
  653.6 12.0 %fusion.370 = f32[768,1,12]{2,1,0:T(1,128)S(1)} fusion(f32[768,56,1]{1,2,0:T(1,128)S(1)} %bitcast.323, f32[768,56,12]{1,2,0:T(8,128)} %copy.167), kind=kOutput, calls=%fused_computation.444.clone.1 | convolution fusion | flops 6193152 | bytes 2273280 | tf_op jit(solution)/shard_map/while/body/eval_jaxpr/sz,sy,syz->s/dot_general | solution.py:293
  691.8 12.6 %fusion.369 = f32[768,1,12]{2,1,0:T(1,128)} fusion(f32[768,56,1]{1,2,0:T(1,128)S(1)} %bitcast.322, f32[768,56,12]{1,2,0:T(8,128)} %copy.169), kind=kOutput, calls=%fused_computation.446.clone.1 | convolution fusion | flops 6193152 | bytes 2273280 | tf_op jit(solution)/shard_map/while/body/eval_jaxpr/sz,sy,syz->s/dot_general | solution.py:295
  713.4 12.0 %fusion.368 = f32[768,1,12]{2,1,0:T(1,128)S(1)} fusion(f32[768,56,1]{1,2,0:T(1,128)S(1)} %bitcast.325, f32[768,56,12]{1,2,0:T(8,128)} %copy.167), kind=kOutput, calls=%fused_computation.445.clone.1 | convolution fusion | flops 6193152 | bytes 2273280 | tf_op jit(solution)/shard_map/while/body/eval_jaxpr/sz,sy,syz->s/dot_general | solution.py:294
  726.8 12.0 %fusion.370 = f32[768,1,12]{2,1,0:T(1,128)S(1)} fusion(f32[768,56,1]{1,2,0:T(1,128)S(1)} %bitcast.323, f32[768,56,12]{1,2,0:T(8,128)} %copy.167), kind=kOutput, calls=%fused_computation.444.clone.1 | convolution fusion | flops 6193152 | bytes 2273280 | tf_op jit(solution)/shard_map/while/body/eval_jaxpr/sz,sy,syz->s/dot_general | solution.py:293
  (360 shorter events, 401.9 us)
Async XLA Ops:
  31.3 7.0 copy-start.23
  56.3 7.0 copy-start.23
  81.3 7.0 copy-start.23
  106.2 7.1 copy-start.23
  113.3 5.3 copy-start.8
  114.5 10.5 %collective-permute-start = (f32[4,56,384]{2,1,0:T(8,128)S(1)}, f32[4,56,384]{2,1,0:T(8,128)S(1)}, u32[]{:S(2)}, u32[]{:S(2)}) collective-permute-start(f32[4,56,384]{2,1,0:T(8,128)S(1)} %get-tuple-element.502), channel_id=1, source_target_pairs={{0,4},{4,8},{8,12},{12,16},{16,20},{20,24},{24,28},{28,0},{1,5},{5... | collective-permute-start | bytes 1032200 | tf_op jit(solution)/shard_map/ppermute | solution.py:26
  114.6 11.5 %collective-permute-start.1 = (f32[4,56,384]{2,1,0:T(8,128)S(1)}, f32[4,56,384]{2,1,0:T(8,128)S(1)}, u32[]{:S(2)}, u32[]{:S(2)}) collective-permute-start(f32[4,56,384]{2,1,0:T(8,128)S(1)} %get-tuple-element.501), channel_id=1, source_target_pairs={{4,0},{8,4},{12,8},{16,12},{20,16},{24,20},{28,24},{0,28},{5,1},{9... | collective-permute-start | bytes 1032200 | tf_op jit(solution)/shard_map/ppermute | solution.py:28
  126.2 4.7 collective-permute-start.2
  129.2 4.9 collective-permute-start.3
  145.5 5.9 copy-start.17
  145.5 29.4 %all-to-all-start = ((f32[4,1,75264]{2,1,0:T(1,128)}), f32[4,1,75264]{2,1,0:T(1,128)S(1)}, u32[]{:S(2)}, u32[]{:S(2)}) async-start(f32[4,1,75264]{2,1,0:T(1,128)} %reshape.1131), calls=%async_computation | async-start | bytes 2408448 | tf_op jit(solution)/shard_map/all_to_all | solution.py:252
  217.9 21.4 %all-to-all-start.1 = ((f32[8,1,37632]{2,1,0:T(1,128)}), f32[8,1,37632]{2,1,0:T(1,128)S(1)}, u32[]{:S(2)}, u32[]{:S(2)}) async-start(f32[8,1,37632]{2,1,0:T(1,128)} %reshape.1133), calls=%async_computation.1 | async-start | bytes 2408448 | tf_op jit(solution)/shard_map/all_to_all | solution.py:255
  327.8 32.6 %all-to-all-start.3 = ((f32[4,1,75264]{2,1,0:T(1,128)}), f32[4,1,75264]{2,1,0:T(1,128)S(1)}, u32[]{:S(2)}, u32[]{:S(2)}) async-start(f32[4,1,75264]{2,1,0:T(1,128)} %reshape.1137), calls=%async_computation.3 | async-start | bytes 2408448 | tf_op jit(solution)/shard_map/all_to_all | solution.py:278
  385.7 13.3 %copy-start.9 = (f32[4,768]{1,0:T(4,128)S(1)}, f32[4,768]{1,0:T(4,128)}, u32[]{:S(2)}) copy-start(f32[4,768]{1,0:T(4,128)} %get-tuple-element.842) | copy-start | bytes 36868
  385.9 9.2 %collective-permute-start.4 = (f32[48,4,384]{2,1,0:T(4,128)S(1)}, f32[48,4,384]{2,1,0:T(4,128)S(1)}, u32[]{:S(2)}, u32[]{:S(2)}) collective-permute-start(f32[48,4,384]{2,1,0:T(4,128)S(1)} %get-tuple-element.509), channel_id=1, source_target_pairs={{0,4},{4,8},{8,12},{12,16},{16,20},{20,24},{24,28},{28,0},{1,5},{5... | collective-permute-start | bytes 884744 | tf_op jit(solution)/shard_map/ppermute | solution.py:26
  385.9 9.1 %collective-permute-start.5 = (f32[48,4,384]{2,1,0:T(4,128)S(1)}, f32[48,4,384]{2,1,0:T(4,128)S(1)}, u32[]{:S(2)}, u32[]{:S(2)}) collective-permute-start(f32[48,4,384]{2,1,0:T(4,128)S(1)} %get-tuple-element.510), channel_id=1, source_target_pairs={{4,0},{8,4},{12,8},{16,12},{20,16},{24,20},{28,24},{0,28},{5,1},{9... | collective-permute-start | bytes 884744 | tf_op jit(solution)/shard_map/ppermute | solution.py:28
  395.1 49.1 %collective-permute-start.6 = (f32[4,24,384]{2,1,0:T(8,128)S(1)}, f32[4,24,384]{2,1,0:T(8,128)S(1)}, u32[]{:S(2)}, u32[]{:S(2)}) collective-permute-start(f32[4,24,384]{2,1,0:T(8,128)S(1)} %get-tuple-element.503), channel_id=1, source_target_pairs={{0,1},{1,2},{2,3},{3,0},{4,5},{5,6},{6,7},{7,4},{8,9},{9,10},{10,1... | collective-permute-start | bytes 442376 | tf_op jit(solution)/shard_map/ppermute | solution.py:26
  396.6 47.6 %collective-permute-start.7 = (f32[4,24,384]{2,1,0:T(8,128)S(1)}, f32[4,24,384]{2,1,0:T(8,128)S(1)}, u32[]{:S(2)}, u32[]{:S(2)}) collective-permute-start(f32[4,24,384]{2,1,0:T(8,128)S(1)} %get-tuple-element.504), channel_id=1, source_target_pairs={{1,0},{2,1},{3,2},{0,3},{5,4},{6,5},{7,6},{4,7},{9,8},{10,9},{11,1... | collective-permute-start | bytes 442376 | tf_op jit(solution)/shard_map/ppermute | solution.py:28
  445.8 293.8 %copy-start.10 = (f32[1536,3]{0,1:T(4,128)S(1)}, f32[1536,3]{0,1:T(4,128)}, u32[]{:S(2)}) copy-start(f32[1536,3]{0,1:T(4,128)} %get-tuple-element.522) | copy-start | bytes 55300
  445.8 293.8 %copy-start.15 = (bf16[3,256]{1,0:T(4,128)(2,1)S(1)}, bf16[3,256]{1,0:T(4,128)(2,1)}, u32[]{:S(2)}) copy-start(bf16[3,256]{1,0:T(4,128)(2,1)} %param.37) | copy-start | bytes 4612
  493.6 13.1 %copy-start.1 = (f32[768,1,12]{2,1,0:T(1,128)S(1)}, f32[768,1,12]{2,1,0:T(1,128)}, u32[]{:S(2)}) copy-start(f32[768,1,12]{2,1,0:T(1,128)} %fusion.369) | copy-start | bytes 110596 | tf_op jit(solution)/shard_map/while
  567.0 13.1 %copy-start.1 = (f32[768,1,12]{2,1,0:T(1,128)S(1)}, f32[768,1,12]{2,1,0:T(1,128)}, u32[]{:S(2)}) copy-start(f32[768,1,12]{2,1,0:T(1,128)} %fusion.369) | copy-start | bytes 110596 | tf_op jit(solution)/shard_map/while
  640.2 13.1 %copy-start.1 = (f32[768,1,12]{2,1,0:T(1,128)S(1)}, f32[768,1,12]{2,1,0:T(1,128)}, u32[]{:S(2)}) copy-start(f32[768,1,12]{2,1,0:T(1,128)} %fusion.369) | copy-start | bytes 110596 | tf_op jit(solution)/shard_map/while
  713.4 13.1 %copy-start.1 = (f32[768,1,12]{2,1,0:T(1,128)S(1)}, f32[768,1,12]{2,1,0:T(1,128)}, u32[]{:S(2)}) copy-start(f32[768,1,12]{2,1,0:T(1,128)} %fusion.369) | copy-start | bytes 110596 | tf_op jit(solution)/shard_map/while
  (20 other events, 38.9 us)
where the time goes:
time: 760 us; the launch traced here: 749 us
  matrix products  254 us (33%)
  local copies, waits for them, and re-layouts  231 us (30%)
  other arithmetic  79.9 us (11%)
  waiting for transfers between devices  79 us (10%)
  blocking collectives  63.9 us (8%)
  starting transfers between devices  29.8 us (4%)
    reduce_sum x12, other arithmetic, dense_window(): jnp.sum(jnp.where(matches, spline_slope[:, :, None], 0.0), axis=1)  53.9 us
    dot_general x4, matrix products, sample_step(): jnp.einsum('sz,sy,syz->s', plane_val, row_val, across, precision=highest)  50.6 us
    dot_general x4, matrix products, sample_step(): jnp.einsum('sz,sy,syz->s', plane_val, row_slope, along, precision=highest)  48.1 us
    dot_general x4, matrix products, sample_step(): jnp.einsum('sz,sy,syz->s', plane_slope, row_val, along, precision=highest)  47.9 us
    unnamed x52, local copies, waits for them, and re-layouts  45 us
    psum x1, blocking collectives, body(): energy_sum = lax.psum(energy_terms, ('slab', 'pencil'))  44.4 us
    reshape x8, local copies, waits for them, and re-layouts, sample_step(): across = both[site_count:].reshape(site_count, CY + 8, BZ + 8)  40.4 us
    dot_general x17, matrix products, lead_product(): lax.dot_general(table, data, (((1,), (dim,)), ((), ())), precision=highest)  39.6 us
  transfers between devices with their start and end apart: 11, of which 7 were waited for; matrix products, arithmetic and copies ran while one was open for 1% of the time, Pallas kernels for 0%

commit v1 on v0

--- a/solution.py
+++ b/solution.py
@@ -3,6 +3,7 @@
 import jax.numpy as jnp
 from jax import lax
 from jax.sharding import PartitionSpec as P
+from jax.lax import axis_index, ppermute, psum
 
 NX = 384
 CZ = 16
@@ -14,6 +15,28 @@
 ewald_beta = 1.4
 shift_scale = 0.9
 highest = lax.Precision.HIGHEST
+
+
+def refer_the_layers_all(arr_in, dimension_no, inner_x):
+    lower = arr_in.shape
+    return jnp.moveaxis(
+        arr_in.reshape(
+            *lower[:dimension_no],
+            inner_x,
+            lower[dimension_no] // inner_x,
+            *lower[dimension_no + 1 :]
+        ),
+        dimension_no,
+        0,
+    )
+
+
+def region_produce(xin, axis_no):
+    xin = jnp.moveaxis(xin, 0, axis_no)
+    wide_out = xin.shape
+    return xin.reshape(
+        *wide_out[:axis_no], wide_out[axis_no] * wide_out[axis_no + 1], *wide_out[axis_no + 2 :]
+    )
 
 
 def extended(cells, sides, width):
@@ -249,7 +272,20 @@
     spectrum = lead_product(forward_rows, source_grid, 2).reshape(
         wave_cols, 2, plane_here, row_here
     )
-    spectrum = lax.all_to_all(spectrum, "pencil", split_axis=0, concat_axis=3, tiled=True)
+    current_arr = psum(1, "pencil")
+    k_now = axis_index("pencil")
+    seen_now, oldest = (current_arr, k_now)
+    prior = refer_the_layers_all(spectrum, 0, seen_now)
+    t = 1
+    items = [prior[oldest]]
+    while t < seen_now:
+        spare = prior[oldest ^ t]
+        tall = ppermute(spare, "pencil", [(j, j ^ t) for j in range(seen_now)])
+        items.append(tall)
+        t = t + 1
+    value_now = jnp.stack(items)
+    prior = value_now[oldest ^ jnp.arange(seen_now)]
+    spectrum = region_produce(prior, 3)
     real_y, imag_y = forward_pair(row_cos, row_sin, spectrum[:, 0], spectrum[:, 1], 2)
     spectrum = jnp.stack([real_y, imag_y], axis=1)
     spectrum = lax.all_to_all(spectrum, "slab", split_axis=0, concat_axis=3, tiled=True)

time: 760 us -> 778 us (1.024)
  waiting for transfers between devices: 79 us -> 113 us
  local copies, waits for them, and re-layouts: 231 us -> 215 us
    ppermute x0 -> x3, waiting for transfers between devices: none -> 66 us  [body(): tall = ppermute(spare, 'pencil', [(j, j ^ t) for j in range(seen_now)])]
    all_to_all x1 -> x0, waiting for transfers between devices: 23.2 us -> none  [body(): lax.all_to_all(spectrum, 'pencil', split_axis=0, concat_axis=3, tiled=True)]
    all_to_all x3 -> x0, local copies, waits for them, and re-layouts: 18.8 us -> none  [body(): lax.all_to_all(spectrum, 'pencil', split_axis=0, concat_axis=3, tiled=True)]
    unnamed x52 -> x50, local copies, waits for them, and re-layouts: 45 us -> 36.4 us
    all_to_all x1, waiting for transfers between devices: 15.1 us -> 6.77 us  [body(): lax.all_to_all(spectrum, 'slab', split_axis=0, concat_axis=3, tiled=True)]
    reshape x0 -> x2, local copies, waits for them, and re-layouts: none -> 8.27 us  [region_produce(): xin.reshape(*wide_out[:axis_no], wide_out[axis_no] * wide_out[axis_no + 1...]
    all_to_all x1, starting transfers between devices: 6.01 us -> 14.2 us  [body(): lax.all_to_all(spectrum, 'slab', split_axis=0, concat_axis=3, tiled=True)]
  transfers between devices with their start and end apart: 11 -> 13, of which waited for: 7 -> 9; matrix products, arithmetic and copies ran while one was open for 1% -> 1% of each run, Pallas kernels for 0% -> 0%
where the time goes in v1:
time: 778 us; the launch traced here: 767 us
  matrix products  255 us (33%)
  local copies, waits for them, and re-layouts  215 us (28%)
  waiting for transfers between devices  113 us (15%)
  other arithmetic  77.9 us (10%)
  blocking collectives  63.9 us (8%)
  starting transfers between devices  31.6 us (4%)
    ppermute x3, waiting for transfers between devices, body(): tall = ppermute(spare, 'pencil', [(j, j ^ t) for j in range(seen_now)])  66 us
    reduce_sum x12, other arithmetic, dense_window(): jnp.sum(jnp.where(matches, spline_slope[:, :, None], 0.0), axis=1)  53.9 us
    dot_general x4, matrix products, sample_step(): jnp.einsum('sz,sy,syz->s', plane_val, row_val, across, precision=highest)  50.6 us
    dot_general x4, matrix products, sample_step(): jnp.einsum('sz,sy,syz->s', plane_val, row_slope, along, precision=highest)  48.1 us
    dot_general x4, matrix products, sample_step(): jnp.einsum('sz,sy,syz->s', plane_slope, row_val, along, precision=highest)  47.9 us
    psum x1, blocking collectives, body(): energy_sum = lax.psum(energy_terms, ('slab', 'pencil'))  44.4 us
    dot_general x17, matrix products, lead_product(): lax.dot_general(table, data, (((1,), (dim,)), ((), ())), precision=highest)  40.8 us
    reshape x8, local copies, waits for them, and re-layouts, sample_step(): across = both[site_count:].reshape(site_count, CY + 8, BZ + 8)  40.4 us
  transfers between devices with their start and end apart: 13, of which 9 were waited for; matrix products, arithmetic and copies ran while one was open for 1% of the time, Pallas kernels for 0%

profile of v1, /device:TPU:12, one launch (start us, length us, event | category | flops | bytes accessed | tf_op | source)
XLA Modules:
  0.0 767.3 jit_solution(7986830021628021637)
XLA Ops:
  13.4 99.9 %while.39 = (s32[]{:T(128)}, f32[24,56,384]{2,1,0:T(8,128)}, f32[4,768,12]{1,2,0:T(8,128)S(1)}, f32[4,768,12]{1,2,0:T(8,128)}, f32[4,768,56]{1,2,0:T(8,128)}, /*...) while((s32[]{:T(128)}, f32[24,56,384]{2,1,0:T(8,128)}, ...), condition=%wide.region_9.10_spmd, body=%wide.region_2.9_spmd.sunk | while | flops 2392848384 | bytes 12563475 | solution.py:250
  15.5 13.0 %select_reduce_fusion.11 = (f32[768,384]{1,0:T(8,128)S(1)}, f32[768,384]{1,0:T(8,128)S(1)}) fusion(f32[768,8]{1,0:T(8,128)S(1)} %copy.152, s32[768,8]{1,0:T(8,128)S(1)} %copy.153, f32[768,8]{1,0:T(8,128)S(1)} %copy.154), kind=kLoop, calls=%fused_computation.18.clone.1 | loop fusion | flops 11206656 | bytes 2433024 | tf_op jit(solution)/shard_map/while/body/eval_jaxpr/reduce_sum | solution.py:152
  40.4 13.0 %select_reduce_fusion.11 = (f32[768,384]{1,0:T(8,128)S(1)}, f32[768,384]{1,0:T(8,128)S(1)}) fusion(f32[768,8]{1,0:T(8,128)S(1)} %copy.152, s32[768,8]{1,0:T(8,128)S(1)} %copy.153, f32[768,8]{1,0:T(8,128)S(1)} %copy.154), kind=kLoop, calls=%fused_computation.18.clone.1 | loop fusion | flops 11206656 | bytes 2433024 | tf_op jit(solution)/shard_map/while/body/eval_jaxpr/reduce_sum | solution.py:152
  65.4 13.0 %select_reduce_fusion.11 = (f32[768,384]{1,0:T(8,128)S(1)}, f32[768,384]{1,0:T(8,128)S(1)}) fusion(f32[768,8]{1,0:T(8,128)S(1)} %copy.152, s32[768,8]{1,0:T(8,128)S(1)} %copy.153, f32[768,8]{1,0:T(8,128)S(1)} %copy.154), kind=kLoop, calls=%fused_computation.18.clone.1 | loop fusion | flops 11206656 | bytes 2433024 | tf_op jit(solution)/shard_map/while/body/eval_jaxpr/reduce_sum | solution.py:152
  90.4 13.0 %select_reduce_fusion.11 = (f32[768,384]{1,0:T(8,128)S(1)}, f32[768,384]{1,0:T(8,128)S(1)}) fusion(f32[768,8]{1,0:T(8,128)S(1)} %copy.152, s32[768,8]{1,0:T(8,128)S(1)} %copy.153, f32[768,8]{1,0:T(8,128)S(1)} %copy.154), kind=kLoop, calls=%fused_computation.18.clone.1 | loop fusion | flops 11206656 | bytes 2433024 | tf_op jit(solution)/shard_map/while/body/eval_jaxpr/reduce_sum | solution.py:152
  143.5 27.1 %collective-permute-done.4 = f32[49,2,16,48]{0,3,2,1:T(8,128)S(1)} collective-permute-done((f32[49,2,16,48]{0,3,2,1:T(8,128)S(1)}, f32[49,2,16,48]{0,3,2,1:T(8,128)S(1)}, u32[]{:S(2)}, u32[]{:S(2)}) %collective-permute-start.4) | collective-permute-done | bytes 301088 | tf_op jit(solution)/shard_map/ppermute | solution.py:283
  170.6 23.8 %collective-permute-done.5 = f32[49,2,16,48]{0,3,2,1:T(8,128)S(1)} collective-permute-done((f32[49,2,16,48]{0,3,2,1:T(8,128)S(1)}, f32[49,2,16,48]{0,3,2,1:T(8,128)S(1)}, u32[]{:S(2)}, u32[]{:S(2)}) %collective-permute-start.5) | collective-permute-done | bytes 301088 | tf_op jit(solution)/shard_map/ppermute | solution.py:283
  194.5 15.1 %collective-permute-done.6 = f32[49,2,16,48]{0,3,2,1:T(8,128)S(1)} collective-permute-done((f32[49,2,16,48]{0,3,2,1:T(8,128)S(1)}, f32[49,2,16,48]{0,3,2,1:T(8,128)S(1)}, u32[]{:S(2)}, u32[]{:S(2)}) %collective-permute-start.6) | collective-permute-done | bytes 301088 | tf_op jit(solution)/shard_map/ppermute | solution.py:283
  239.7 14.2 %all-to-all-start = ((f32[8,1,37632]{2,1,0:T(1,128)}), f32[8,1,37632]{2,1,0:T(1,128)S(1)}, u32[]{:S(2)}, u32[]{:S(2)}) async-start(f32[8,1,37632]{2,1,0:T(1,128)} %reshape.1154), calls=%async_computation | async-start | bytes 2408448 | tf_op jit(solution)/shard_map/all_to_all | solution.py:291
  296.6 19.5 %all_to_all.54 = f32[8,1,37632]{2,1,0:T(1,128)S(1)} all-to-all(f32[8,1,37632]{2,1,0:T(1,128)S(1)} %reshape.1156), channel_id=1, replica_groups=mesh['slab'=8,'pencil'=4] {'slab'}, dimensions={0} | all-to-all | bytes 2408448 | tf_op jit(solution)/shard_map/all_to_all | solution.py:311
  355.4 24.1 %all-to-all-done.2 = f32[4,1,75264]{2,1,0:T(1,128)S(1)} async-done(((f32[4,1,75264]{2,1,0:T(1,128)}), f32[4,1,75264]{2,1,0:T(1,128)S(1)}, u32[]{:S(2)}, u32[]{:S(2)}) %all-to-all-start.2) | async-done | bytes 1204256 | tf_op jit(solution)/shard_map/all_to_all | solution.py:314
  417.2 44.4 %psum.7 = f32[]{:T(128)} all-reduce(f32[]{:T(128)S(6)} %mul_shard_map.3), channel_id=1, replica_groups=mesh['slab'=8,'pencil'=4] {'slab','pencil'}, use_global_device_ids=true, to_apply=%region_17.18 | all-reduce | flops 1 | bytes 8 | tf_op jit(solution)/shard_map/psum | solution.py:308
  463.9 293.6 %while.40 = (s32[]{:T(128)}, f32[4,3,768]{2,1,0:T(4,128)S(1)}, f32[4,768,12]{1,2,0:T(8,128)}, f32[4,768,56]{1,2,0:T(8,128)}, f32[4,768,384]{2,1,0:T(8,128)}, /*i...) while((s32[]{:T(128)}, f32[4,3,768]{2,1,0:T(4,128)S(1)}, ...), condition=%wide.region_19.20_spmd, body=%wide.region_18.19_spmd.sunk | while | flops 4775567872 | bytes 50012400 | solution.py:334
  490.1 12.6 %fusion.370 = f32[768,1,12]{2,1,0:T(1,128)} fusion(f32[768,56,1]{1,2,0:T(1,128)S(1)} %bitcast.334, f32[768,56,12]{1,2,0:T(8,128)} %copy.159), kind=kOutput, calls=%fused_computation.456.clone.1 | convolution fusion | flops 6193152 | bytes 2273280 | tf_op jit(solution)/shard_map/while/body/eval_jaxpr/sz,sy,syz->s/dot_general | solution.py:331
  511.7 12.0 %fusion.369 = f32[768,1,12]{2,1,0:T(1,128)S(1)} fusion(f32[768,56,1]{1,2,0:T(1,128)S(1)} %bitcast.337, f32[768,56,12]{1,2,0:T(8,128)} %copy.157), kind=kOutput, calls=%fused_computation.455.clone.1 | convolution fusion | flops 6193152 | bytes 2273280 | tf_op jit(solution)/shard_map/while/body/eval_jaxpr/sz,sy,syz->s/dot_general | solution.py:330
  525.1 12.0 %fusion.371 = f32[768,1,12]{2,1,0:T(1,128)S(1)} fusion(f32[768,56,1]{1,2,0:T(1,128)S(1)} %bitcast.335, f32[768,56,12]{1,2,0:T(8,128)} %copy.157), kind=kOutput, calls=%fused_computation.454.clone.1 | convolution fusion | flops 6193152 | bytes 2273280 | tf_op jit(solution)/shard_map/while/body/eval_jaxpr/sz,sy,syz->s/dot_general | solution.py:329
  563.6 12.6 %fusion.370 = f32[768,1,12]{2,1,0:T(1,128)} fusion(f32[768,56,1]{1,2,0:T(1,128)S(1)} %bitcast.334, f32[768,56,12]{1,2,0:T(8,128)} %copy.159), kind=kOutput, calls=%fused_computation.456.clone.1 | convolution fusion | flops 6193152 | bytes 2273280 | tf_op jit(solution)/shard_map/while/body/eval_jaxpr/sz,sy,syz->s/dot_general | solution.py:331
  585.2 12.0 %fusion.369 = f32[768,1,12]{2,1,0:T(1,128)S(1)} fusion(f32[768,56,1]{1,2,0:T(1,128)S(1)} %bitcast.337, f32[768,56,12]{1,2,0:T(8,128)} %copy.157), kind=kOutput, calls=%fused_computation.455.clone.1 | convolution fusion | flops 6193152 | bytes 2273280 | tf_op jit(solution)/shard_map/while/body/eval_jaxpr/sz,sy,syz->s/dot_general | solution.py:330
  598.5 12.0 %fusion.371 = f32[768,1,12]{2,1,0:T(1,128)S(1)} fusion(f32[768,56,1]{1,2,0:T(1,128)S(1)} %bitcast.335, f32[768,56,12]{1,2,0:T(8,128)} %copy.157), kind=kOutput, calls=%fused_computation.454.clone.1 | convolution fusion | flops 6193152 | bytes 2273280 | tf_op jit(solution)/shard_map/while/body/eval_jaxpr/sz,sy,syz->s/dot_general | solution.py:329
  636.8 12.6 %fusion.370 = f32[768,1,12]{2,1,0:T(1,128)} fusion(f32[768,56,1]{1,2,0:T(1,128)S(1)} %bitcast.334, f32[768,56,12]{1,2,0:T(8,128)} %copy.159), kind=kOutput, calls=%fused_computation.456.clone.1 | convolution fusion | flops 6193152 | bytes 2273280 | tf_op jit(solution)/shard_map/while/body/eval_jaxpr/sz,sy,syz->s/dot_general | solution.py:331
  658.4 12.0 %fusion.369 = f32[768,1,12]{2,1,0:T(1,128)S(1)} fusion(f32[768,56,1]{1,2,0:T(1,128)S(1)} %bitcast.337, f32[768,56,12]{1,2,0:T(8,128)} %copy.157), kind=kOutput, calls=%fused_computation.455.clone.1 | convolution fusion | flops 6193152 | bytes 2273280 | tf_op jit(solution)/shard_map/while/body/eval_jaxpr/sz,sy,syz->s/dot_general | solution.py:330
  710.0 12.6 %fusion.370 = f32[768,1,12]{2,1,0:T(1,128)} fusion(f32[768,56,1]{1,2,0:T(1,128)S(1)} %bitcast.334, f32[768,56,12]{1,2,0:T(8,128)} %copy.159), kind=kOutput, calls=%fused_computation.456.clone.1 | convolution fusion | flops 6193152 | bytes 2273280 | tf_op jit(solution)/shard_map/while/body/eval_jaxpr/sz,sy,syz->s/dot_general | solution.py:331
  731.6 12.0 %fusion.369 = f32[768,1,12]{2,1,0:T(1,128)S(1)} fusion(f32[768,56,1]{1,2,0:T(1,128)S(1)} %bitcast.337, f32[768,56,12]{1,2,0:T(8,128)} %copy.157), kind=kOutput, calls=%fused_computation.455.clone.1 | convolution fusion | flops 6193152 | bytes 2273280 | tf_op jit(solution)/shard_map/while/body/eval_jaxpr/sz,sy,syz->s/dot_general | solution.py:330
  744.9 12.0 %fusion.371 = f32[768,1,12]{2,1,0:T(1,128)S(1)} fusion(f32[768,56,1]{1,2,0:T(1,128)S(1)} %bitcast.335, f32[768,56,12]{1,2,0:T(8,128)} %copy.157), kind=kOutput, calls=%fused_computation.454.clone.1 | convolution fusion | flops 6193152 | bytes 2273280 | tf_op jit(solution)/shard_map/while/body/eval_jaxpr/sz,sy,syz->s/dot_general | solution.py:329
  (366 shorter events, 401.4 us)
Async XLA Ops:
  31.3 7.0 copy-start.23
  56.3 7.0 copy-start.23
  81.3 7.0 copy-start.23
  106.2 7.1 copy-start.23
  115.3 10.9 %collective-permute-start = (f32[4,56,384]{2,1,0:T(8,128)}, f32[4,56,384]{2,1,0:T(8,128)S(1)}, u32[]{:S(2)}, u32[]{:S(2)}) collective-permute-start(f32[4,56,384]{2,1,0:T(8,128)} %get-tuple-element.506), channel_id=1, source_target_pairs={{0,4},{4,8},{8,12},{12,16},{16,20},{20,24},{24,28},{28,0},{1,5},{5... | collective-permute-start | bytes 1032200 | tf_op jit(solution)/shard_map/ppermute | solution.py:49
  115.3 11.9 %collective-permute-start.1 = (f32[4,56,384]{2,1,0:T(8,128)S(1)}, f32[4,56,384]{2,1,0:T(8,128)S(1)}, u32[]{:S(2)}, u32[]{:S(2)}) collective-permute-start(f32[4,56,384]{2,1,0:T(8,128)S(1)} %get-tuple-element.505), channel_id=1, source_target_pairs={{4,0},{8,4},{12,8},{16,12},{20,16},{24,20},{28,24},{0,28},{5,1},{9... | collective-permute-start | bytes 1032200 | tf_op jit(solution)/shard_map/ppermute | solution.py:51
  127.3 5.5 collective-permute-start.2
  129.1 5.3 collective-permute-start.3
  140.0 30.7 %collective-permute-start.4 = (f32[49,2,16,48]{0,3,2,1:T(8,128)S(1)}, f32[49,2,16,48]{0,3,2,1:T(8,128)S(1)}, u32[]{:S(2)}, u32[]{:S(2)}) collective-permute-start(f32[49,2,16,48]{0,3,2,1:T(8,128)S(1)} %get-tuple-element.504), channel_id=1, source_target_pairs={{0,1},{1,0},{2,3},{3,2},{4,5},{5,4},{6,7},{7,6},{8,9},{9,8},{10,11... | collective-permute-start | bytes 903176 | tf_op jit(solution)/shard_map/ppermute | solution.py:283
  141.0 53.5 %collective-permute-start.5 = (f32[49,2,16,48]{0,3,2,1:T(8,128)S(1)}, f32[49,2,16,48]{0,3,2,1:T(8,128)S(1)}, u32[]{:S(2)}, u32[]{:S(2)}) collective-permute-start(f32[49,2,16,48]{0,3,2,1:T(8,128)S(1)} %get-tuple-element.503), channel_id=1, source_target_pairs={{0,2},{1,3},{2,0},{3,1},{4,6},{5,7},{6,4},{7,5},{8,10},{9,11},{10,... | collective-permute-start | bytes 903176 | tf_op jit(solution)/shard_map/ppermute | solution.py:283
  142.8 66.8 %collective-permute-start.6 = (f32[49,2,16,48]{0,3,2,1:T(8,128)S(1)}, f32[49,2,16,48]{0,3,2,1:T(8,128)S(1)}, u32[]{:S(2)}, u32[]{:S(2)}) collective-permute-start(f32[49,2,16,48]{0,3,2,1:T(8,128)S(1)} %get-tuple-element.502), channel_id=1, source_target_pairs={{0,3},{1,2},{2,1},{3,0},{4,7},{5,6},{6,5},{7,4},{8,11},{9,10},{10,... | collective-permute-start | bytes 903176 | tf_op jit(solution)/shard_map/ppermute | solution.py:283
  239.7 21.3 %all-to-all-start = ((f32[8,1,37632]{2,1,0:T(1,128)}), f32[8,1,37632]{2,1,0:T(1,128)S(1)}, u32[]{:S(2)}, u32[]{:S(2)}) async-start(f32[8,1,37632]{2,1,0:T(1,128)} %reshape.1154), calls=%async_computation | async-start | bytes 2408448 | tf_op jit(solution)/shard_map/all_to_all | solution.py:291
  349.8 29.7 %all-to-all-start.2 = ((f32[4,1,75264]{2,1,0:T(1,128)}), f32[4,1,75264]{2,1,0:T(1,128)S(1)}, u32[]{:S(2)}, u32[]{:S(2)}) async-start(f32[4,1,75264]{2,1,0:T(1,128)} %reshape.1158), calls=%async_computation.2 | async-start | bytes 2408448 | tf_op jit(solution)/shard_map/all_to_all | solution.py:314
  404.7 12.5 %copy-start.9 = (f32[4,768]{1,0:T(4,128)S(1)}, f32[4,768]{1,0:T(4,128)}, u32[]{:S(2)}) copy-start(f32[4,768]{1,0:T(4,128)} %get-tuple-element.848) | copy-start | bytes 36868
  404.8 9.2 %collective-permute-start.7 = (f32[48,4,384]{2,1,0:T(4,128)S(1)}, f32[48,4,384]{2,1,0:T(4,128)S(1)}, u32[]{:S(2)}, u32[]{:S(2)}) collective-permute-start(f32[48,4,384]{2,1,0:T(4,128)S(1)} %get-tuple-element.511), channel_id=1, source_target_pairs={{0,4},{4,8},{8,12},{12,16},{16,20},{20,24},{24,28},{28,0},{1,5},{5... | collective-permute-start | bytes 884744 | tf_op jit(solution)/shard_map/ppermute | solution.py:49
  404.9 9.1 %collective-permute-start.8 = (f32[48,4,384]{2,1,0:T(4,128)S(1)}, f32[48,4,384]{2,1,0:T(4,128)S(1)}, u32[]{:S(2)}, u32[]{:S(2)}) collective-permute-start(f32[48,4,384]{2,1,0:T(4,128)S(1)} %get-tuple-element.512), channel_id=1, source_target_pairs={{4,0},{8,4},{12,8},{16,12},{20,16},{24,20},{28,24},{0,28},{5,1},{9... | collective-permute-start | bytes 884744 | tf_op jit(solution)/shard_map/ppermute | solution.py:51
  414.0 48.3 %collective-permute-start.10 = (f32[4,24,384]{2,1,0:T(8,128)S(1)}, f32[4,24,384]{2,1,0:T(8,128)S(1)}, u32[]{:S(2)}, u32[]{:S(2)}) collective-permute-start(f32[4,24,384]{2,1,0:T(8,128)S(1)} %get-tuple-element.508), channel_id=1, source_target_pairs={{1,0},{2,1},{3,2},{0,3},{5,4},{6,5},{7,6},{4,7},{9,8},{10,9},{11,1... | collective-permute-start | bytes 442376 | tf_op jit(solution)/shard_map/ppermute | solution.py:51
  416.6 45.7 %collective-permute-start.9 = (f32[4,24,384]{2,1,0:T(8,128)S(1)}, f32[4,24,384]{2,1,0:T(8,128)S(1)}, u32[]{:S(2)}, u32[]{:S(2)}) collective-permute-start(f32[4,24,384]{2,1,0:T(8,128)S(1)} %get-tuple-element.507), channel_id=1, source_target_pairs={{0,1},{1,2},{2,3},{3,0},{4,5},{5,6},{6,7},{7,4},{8,9},{9,10},{10,1... | collective-permute-start | bytes 442376 | tf_op jit(solution)/shard_map/ppermute | solution.py:49
  463.9 293.8 %copy-start.10 = (f32[1536,3]{0,1:T(4,128)S(1)}, f32[1536,3]{0,1:T(4,128)}, u32[]{:S(2)}) copy-start(f32[1536,3]{0,1:T(4,128)} %get-tuple-element.524) | copy-start | bytes 55300
  463.9 293.8 %copy-start.15 = (bf16[3,256]{1,0:T(4,128)(2,1)S(1)}, bf16[3,256]{1,0:T(4,128)(2,1)}, u32[]{:S(2)}) copy-start(bf16[3,256]{1,0:T(4,128)(2,1)} %param.37) | copy-start | bytes 4612
  511.7 13.1 %copy-start.1 = (f32[768,1,12]{2,1,0:T(1,128)S(1)}, f32[768,1,12]{2,1,0:T(1,128)}, u32[]{:S(2)}) copy-start(f32[768,1,12]{2,1,0:T(1,128)} %fusion.370) | copy-start | bytes 110596 | tf_op jit(solution)/shard_map/while
  585.1 13.1 %copy-start.1 = (f32[768,1,12]{2,1,0:T(1,128)S(1)}, f32[768,1,12]{2,1,0:T(1,128)}, u32[]{:S(2)}) copy-start(f32[768,1,12]{2,1,0:T(1,128)} %fusion.370) | copy-start | bytes 110596 | tf_op jit(solution)/shard_map/while
  658.4 13.1 %copy-start.1 = (f32[768,1,12]{2,1,0:T(1,128)S(1)}, f32[768,1,12]{2,1,0:T(1,128)}, u32[]{:S(2)}) copy-start(f32[768,1,12]{2,1,0:T(1,128)} %fusion.370) | copy-start | bytes 110596 | tf_op jit(solution)/shard_map/while
  731.6 13.1 %copy-start.1 = (f32[768,1,12]{2,1,0:T(1,128)S(1)}, f32[768,1,12]{2,1,0:T(1,128)}, u32[]{:S(2)}) copy-start(f32[768,1,12]{2,1,0:T(1,128)} %fusion.370) | copy-start | bytes 110596 | tf_op jit(solution)/shard_map/while
  (22 other events, 51.1 us)
